TPU v7x, 32 devices: a whole 2x2x4 slice. The times are simulated.
32 devices in a mesh: store: 4 (over x, core), blk: 2 (over y), batch: 4 (over z).
Axes of the slice: x: 2, y: 2, z: 4, core: 2. Of those that a mesh axis runs over, the one named last changes fastest.
Arguments:
- cands: bfloat16 [16, 256, 1024], P(('batch', 'store'), 'blk'), parts along dimension 0, may hold values from -6 to 6
- kv_store: bfloat16 [16, 512, 2, 1024], P('batch', ('blk', 'store')), parts along dimension 0, may hold values from -6 to 6
- proj_weight: bfloat16 [1024, 2, 1024], P(None, None, 'blk'), may hold values from -0.1875 to 0.1875
- norm_gain: float32 [1024], replicated, may hold values from 0.5 to 1.5
- users: int32 [16], P('batch'), parts along dimension 0, may hold values from 0 to 3, each once
- lengths: int32 [16], P('batch'), parts along dimension 0, may hold values from 128 to 512, as said below
Outputs:
- scored: bfloat16 [16, 256, 1024], P(('batch', 'store'), 'blk'), parts along dimension 0
There are 4 independent parts, one for each index of `batch`. A program takes and returns all parts, laid end to end along the dimension named above; an argument that names none is the same for every part. Nothing has to cross between parts.
Inputs may be any that keep to these rules, and one draw needn't show every extreme that they name: A permutation of the users. `lengths`: some user has all 512 events live.
All inputs are finite; a program needn't handle non-finite values.
Results may differ from a plain program's by a relative error of at most 0.014.
Values may be sent and summed in bfloat16 or wider, within the bound.
No kernel may reach another device: no remote copies, remote signals or barrier semaphores. Data moves between devices by JAX's collectives and lax.ppermute only.
A program may use at most 64 MiB of HBM per device.

v0:
```python
import jax
import jax.numpy as jnp
from jax import lax
from jax.sharding import PartitionSpec as P
from jax.experimental.layout import Layout, with_layout_constraint

D = 1024
HEADS = 8
HEAD_SIZE = D // HEADS


def attend(qheads, keys, values, count):
    inverse = HEAD_SIZE ** (-0.5)
    local_heads, rows, _ = qheads.shape
    total = keys.shape[1]
    block = min(total, 512)
    scale_count = count.astype(jnp.float32)

    def one_block(index, accum):
        start = index * block
        key_block = lax.dynamic_slice_in_dim(keys, start, block, 1)
        value_block = lax.dynamic_slice_in_dim(values, start, block, 1)
        scores = (
            jnp.einsum("hcd,hkd->hck", qheads, key_block, preferred_element_type=jnp.float32)
            * inverse
        )
        live = (start + jnp.arange(block) < count).astype(jnp.float32)
        weights = (jax.nn.silu(scores) * live[None, None, :] / scale_count).astype(jnp.bfloat16)
        part_sum = jnp.einsum(
            "hck,hkd->chd", weights, value_block, preferred_element_type=jnp.float32
        )
        return accum + part_sum.reshape(rows, local_heads * HEAD_SIZE)

    empty = jnp.zeros((rows, local_heads * HEAD_SIZE), jnp.float32)
    steps = total // block
    if steps == 1:
        return one_block(0, empty)
    return lax.fori_loop(0, steps, one_block, empty)


def finish(attended, gate, norm_gain):
    wide = attended.astype(jnp.float32)
    mean = jnp.mean(wide, axis=1, keepdims=True)
    var = jnp.mean((wide - mean) ** 2, axis=1, keepdims=True)
    normed = (wide - mean) * lax.rsqrt(var + 1e-05) * norm_gain[None, :]
    return (normed * gate.astype(jnp.float32)).astype(jnp.bfloat16)


def per_device(cands, kv_store, proj_weight, norm_gain, users, lengths):
    n_blk = lax.axis_size("blk")
    blk = lax.axis_index("blk")
    slot = lax.axis_index("store")
    ids = jnp.arange(users.shape[0], dtype=jnp.int32)
    chosen = (ids[:, None] == slot) & (users[:, None] == ids[None, :])
    count = jnp.sum(jnp.where(chosen, lengths[None, :], 0))
    half = proj_weight.shape[2]
    local_heads = half // HEAD_SIZE
    n_users, n_pos = (kv_store.shape[0], kv_store.shape[1])
    ordered = (
        kv_store.at[users]
        .get(mode="promise_in_bounds", unique_indices=True)
        .reshape(n_users, n_pos, 2, n_blk, local_heads, HEAD_SIZE)
    )
    ordered = jnp.transpose(ordered, (3, 0, 2, 4, 1, 5)).reshape(
        n_blk * n_users, 2, local_heads, n_pos, HEAD_SIZE
    )
    fetched = lax.all_to_all(ordered, ("blk", "store"), split_axis=0, concat_axis=3, tiled=True)
    keys = fetched[0, 0]
    values = fetched[0, 1]
    mine = cands[0]
    rows = mine.shape[0]

    def project(feats):
        proj = jnp.einsum("cd,dkh->kch", feats, proj_weight, preferred_element_type=jnp.float32)
        query = proj[0].astype(jnp.bfloat16).reshape(-1, local_heads, HEAD_SIZE)
        gate = jax.nn.silu(proj[1]).astype(jnp.bfloat16)
        return (jnp.transpose(query, (1, 0, 2)), gate)

    if n_blk == 2:
        swap = [(0, 1), (1, 0)]
        peer = lax.ppermute(mine, "blk", swap)
        query_own, gate_own = project(mine)
        query_peer, gate_peer = project(peer)
        gate_back = lax.ppermute(gate_peer, "blk", swap)
        row_major = Layout(major_to_minor=(0, 1))
        sent = attend(query_peer, keys, values, count).astype(jnp.bfloat16)
        sent = with_layout_constraint(sent, row_major)
        back = lax.ppermute(sent, "blk", swap)
        query_own, gate_own, _ = lax.optimization_barrier((query_own, gate_own, sent))
        kept = attend(query_own, keys, values, count).astype(jnp.bfloat16)
        kept = with_layout_constraint(kept, row_major)
        first = blk == 0
        attended = jnp.where(
            first, jnp.concatenate([kept, back], axis=1), jnp.concatenate([back, kept], axis=1)
        )
        gate_full = jnp.where(
            first,
            jnp.concatenate([gate_own, gate_back], axis=1),
            jnp.concatenate([gate_back, gate_own], axis=1),
        )
        return finish(attended, gate_full, norm_gain)[None]
    feats = lax.all_gather(mine, "blk", axis=0, tiled=True)
    query, gate = project(feats)
    attended = attend(query, keys, values, count).astype(jnp.bfloat16)
    both = jnp.stack([attended, gate]).reshape(2, n_blk, rows, half)
    own = lax.all_to_all(both, "blk", split_axis=1, concat_axis=3, tiled=True)
    own = own.reshape(2, rows, n_blk * half)
    return finish(own[0], own[1], norm_gain)[None]


def solution(mesh):
    in_specs = (
        P(("batch", "store"), "blk", None),
        P("batch", ("blk", "store"), None, None),
        P(None, None, "blk"),
        P(),
        P("batch"),
        P("batch"),
    )
    out_specs = P(("batch", "store"), "blk", None)
    return jax.shard_map(
        per_device, mesh=mesh, in_specs=in_specs, out_specs=out_specs, check_vma=False
    )
```

profile of v0, /device:TPU:0, one launch (start us, length us, event | category | flops | bytes accessed | tf_op | source)
XLA Modules:
  0.0 37.3 jit_solution(15497531011760025280)
XLA Ops:
  0.0 3.0 %collective-permute-start = (bf16[128,1024]{1,0:T(8,128)(2,1)}, bf16[128,1024]{1,0:T(8,128)(2,1)}, u32[]{:S(2)}, u32[]{:S(2)}) collective-permute-start(bf16[128,1024]{1,0:T(8,128)(2,1)} %bitcast.66), channel_id=1, source_target_pairs={{0,4},{4,0},{1,5},{5,1},{2,6},{6,2},{3,7},{7,3},{8,12},{12,8},{9,1... | collective-permute-start | bytes 786440 | tf_op jit(solution)/shard_map/ppermute | solution.py:81
  3.0 0.7 %compare_select_fusion = s32[4]{0:T(128)S(1)} fusion(s32[4]{0:T(128)} %param.10), kind=kLoop, calls=%fused_computation.42 | loop fusion | flops 12 | bytes 32 | tf_op jit(solution)/shard_map/select_n | solution.py:61
  3.6 2.7 %gather_fusion = bf16[4,64,2,1024]{3,2,1,0:T(2,128)(2,1)S(1)} fusion(bf16[4,64,2,1024]{3,2,1,0:T(2,128)(2,1)S(1)} %copy-done, s32[1024]{0:T(1024)S(1)} %pad_clamp_fusion), kind=kCustom, calls=%fused_computation | custom fusion | bytes 2097168 | tf_op jit(solution)/shard_map/gather | solution.py:61
  6.3 0.7 %reshape.231 = bf16[4,64,2,2,4,128]{5,4,3,2,1,0:T(4,128)(2,1)S(1)} reshape(bf16[4,64,2,1024]{3,2,1,0:T(2,128)(2,1)S(1)} %gather_fusion) | data formatting | bytes 2097152 | tf_op jit(solution)/shard_map/reshape | solution.py:62
  7.0 1.3 %copy.26 = bf16[4,64,2,2,4,128]{5,1,4,2,0,3:T(8,128)(2,1)} copy(bf16[4,64,2,2,4,128]{5,4,3,2,1,0:T(4,128)(2,1)S(1)} %reshape.231) | data formatting | bytes 2097152 | tf_op jit(solution)/shard_map/reshape | solution.py:62
  8.3 4.2 %all-to-all-start = ((bf16[8,2,4,64,128]{4,3,2,1,0:T(8,128)(2,1)}), bf16[8,2,4,64,128]{4,3,2,1,0:T(8,128)(2,1)}, u32[]{:S(2)}, u32[]{:S(2)}) async-start(bf16[8,2,4,64,128]{4,3,2,1,0:T(8,128)(2,1)} %bitcast.1), calls=%async_computation | async-start | bytes 2097152 | tf_op jit(solution)/shard_map/all_to_all | solution.py:67
  12.6 4.8 %copy.28 = bf16[1024,2,512]{0,2,1:T(8,128)(2,1)S(1)} copy(bf16[1024,2,512]{2,1,0:T(2,128)(2,1)} %param.8) | data formatting | bytes 4194304 | tf_op args[2]
  17.4 1.6 %convolution_bitcast_fusion.1 = f32[2,128,512]{2,1,0:T(8,128)} fusion(bf16[1024,2,512]{0,2,1:T(8,128)(2,1)S(1)} %copy.28, bf16[1,128,1024]{2,1,0:T(8,128)(2,1)S(1)} %copy-done.2), kind=kOutput, calls=%fused_computation.4 | convolution fusion | flops 268435456 | bytes 2883584 | tf_op jit(solution)/shard_map/cd,dkh->kch/dot_general | solution.py:74
  19.0 0.7 %select_reduce_fusion = s32[]{:T(128)} fusion(s32[4]{0:T(128)S(1)} %copy-done.4, s32[4]{0:T(128)S(1)} %copy-done.5, pred[4]{0:T(512)(128)(4,1)S(1)} %iota_compare_fusion.2), kind=kLoop, calls=%fused_computation.43 | loop fusion | flops 63 | bytes 40 | tf_op jit(solution)/shard_map/reduce_sum | solution.py:55
  19.8 0.6 %fusion.17 = f32[512]{0:T(512)S(1)} fusion(s32[]{:T(128)} %select_reduce_fusion), kind=kLoop, calls=%fused_computation.46 | loop fusion | flops 1024 | bytes 2052 | tf_op jit(solution)/shard_map/convert_element_type | solution.py:27
  21.1 1.0 %slice.51 = bf16[1,128,512]{2,1,0:T(8,128)(2,1)S(1)} slice(f32[2,128,512]{2,1,0:T(8,128)} %convolution_bitcast_fusion.1), slice={[0:1], [0:128], [0:512]} | slice | bytes 262144 | tf_op jit(solution)/shard_map/slice | solution.py:75
  22.1 1.0 %multiply_convert_fusion.2 = bf16[128,512]{1,0:T(8,128)(2,1)S(1)} fusion(f32[2,128,512]{2,1,0:T(8,128)} %convolution_bitcast_fusion.1), kind=kLoop, calls=%fused_computation.35 | loop fusion | flops 327680 | bytes 393216 | tf_op jit(solution)/shard_map/convert_element_type | solution.py:76
  23.1 1.8 %convolution_bitcast_fusion = f32[2,128,512]{2,1,0:T(8,128)S(1)} fusion(bf16[1024,2,512]{0,2,1:T(8,128)(2,1)S(1)} %copy.28, bf16[128,1024]{1,0:T(8,128)(2,1)} %collective-permute-done), kind=kOutput, calls=%fused_computation.3 | convolution fusion | flops 268435456 | bytes 2883584 | tf_op jit(solution)/shard_map/cd,dkh->kch/dot_general | solution.py:74
  24.9 0.8 %copy-done.1 = f32[2,128,512]{2,1,0:T(8,128)} copy-done((f32[2,128,512]{2,1,0:T(8,128)}, f32[2,128,512]{2,1,0:T(8,128)S(1)}, u32[]{:S(2)}) %copy-start.1) | copy-done | bytes 524312
  25.8 1.0 %multiply_convert_fusion.1 = bf16[128,512]{1,0:T(8,128)(2,1)S(1)} fusion(f32[2,128,512]{2,1,0:T(8,128)} %copy-done.1), kind=kLoop, calls=%fused_computation.34 | loop fusion | flops 327680 | bytes 393216 | tf_op jit(solution)/shard_map/convert_element_type | solution.py:76
  26.8 2.0 %collective-permute-start.2 = (bf16[128,512]{1,0:T(8,128)(2,1)S(1)}, bf16[128,512]{1,0:T(8,128)(2,1)S(1)}, u32[]{:S(2)}, u32[]{:S(2)}) collective-permute-start(bf16[128,512]{1,0:T(8,128)(2,1)S(1)} %multiply_convert_fusion.1), channel_id=1, source_target_pairs={{0,4},{4,0},{1,5},{5,1},{2,6},{6,2},{3,7},{7,3},{8,12},{12,8},{9,1... | collective-permute-start | bytes 393224 | tf_op jit(solution)/shard_map/ppermute | solution.py:84
  28.8 1.3 %copy.27 = bf16[1,2,4,8,64,128]{5,4,3,2,1,0:T(8,128)(2,1)S(1)} copy(bf16[1,2,4,8,64,128]{5,4,2,1,3,0:T(8,128)(2,1)} %bitcast.3) | data formatting | bytes 2097152 | tf_op jit(solution)/shard_map/all_to_all | solution.py:67
  30.1 0.6 %fusion = bf16[4,16,8,128]{3,2,1,0:T(8,128)(2,1)S(1)} fusion(f32[]{:T(128)S(6)} %convert_element_type.88, f32[512]{0:T(512)S(1)} %fusion.17, bf16[1,2,4,512,128]{4,3,2,1,0:T(8,128)(2,1)S(1)} %bitcast.62, bf16[128,4,128]{2,1,0:T(4,128)(2,1)S(1)} %convert_element_type.86), kind=kOutput, calls=%fused_computation.7 | convolution fusion | flops 136380416 | bytes 1312772 | tf_op jit(solution)/shard_map/hck,hkd->chd/dot_general | solution.py:29
  30.8 0.2 collective-permute-start.1
  31.0 0.6 %convolution_convert_fusion = bf16[4,128,128]{1,2,0:T(8,128)(2,1)S(1)} fusion(bf16[4,128,128]{2,1,0:T(8,128)(2,1)S(1)} %bitcast.67, f32[]{:T(128)S(6)} %convert_element_type.88, f32[512]{0:T(512)S(1)} %fusion.17, bf16[1,2,4,512,128]{4,3,2,1,0:T(8,128)(2,1)S(1)} %bitcast.63), kind=kOutput, calls=%fused_computation.5 | convolution fusion | flops 136380416 | bytes 1312772 | tf_op jit(solution)/shard_map/hck,hkd->chd/dot_general | solution.py:29
  31.8 4.3 %collective-permute-done.1 = bf16[128,512]{1,0:T(8,128)(2,1)S(1)} collective-permute-done((bf16[128,512]{1,0:T(8,128)(2,1)S(1)}, bf16[128,512]{1,0:T(8,128)(2,1)S(1)}, u32[]{:S(2)}, u32[]{:S(2)}) %collective-permute-start.1) | collective-permute-done | bytes 131104 | tf_op jit(solution)/shard_map/ppermute | solution.py:88
  36.1 0.1 convert_reduce_fusion
  36.2 0.2 fusion.2
  36.5 0.9 %multiply_convert_fusion = bf16[1,128,1024]{2,1,0:T(8,128)(2,1)} fusion(bf16[1,128,512]{2,1,0:T(8,128)(2,1)S(1)} %bitcast.61, bf16[1,128,512]{2,1,0:T(8,128)(2,1)S(1)} %concatenate.52, bf16[1,128,512]{2,1,0:T(8,128)(2,1)S(1)} %bitcast.69, bf16[1,128,512]{2,1,0:T(8,128)(2,1)S(1)} %bitcast.64, f32[1024]{0:T(1024)S(1)} %copy-done.3, f32[128]{0:T(128)S(1)} %add_rsqrt_fusion, ...), kind=kLoop, calls=%fused_computation.16 | loop fusion | flops 3276800 | bytes 791553 | tf_op jit(solution)/shard_map/convert_element_type | solution.py:46
  (26 shorter events, 0.4 us)
Async XLA Ops:
  0.0 3.6 %copy-start = (bf16[4,64,2,1024]{3,2,1,0:T(2,128)(2,1)S(1)}, bf16[4,64,2,1024]{3,2,1,0:T(2,128)(2,1)}, u32[]{:S(2)}) copy-start(bf16[4,64,2,1024]{3,2,1,0:T(2,128)(2,1)} %param.7) | copy-start | bytes 3145732
  0.0 23.1 %collective-permute-start = (bf16[128,1024]{1,0:T(8,128)(2,1)}, bf16[128,1024]{1,0:T(8,128)(2,1)}, u32[]{:S(2)}, u32[]{:S(2)}) collective-permute-start(bf16[128,1024]{1,0:T(8,128)(2,1)} %bitcast.66), channel_id=1, source_target_pairs={{0,4},{4,0},{1,5},{5,1},{2,6},{6,2},{3,7},{7,3},{8,12},{12,8},{9,1... | collective-permute-start | bytes 786440 | tf_op jit(solution)/shard_map/ppermute | solution.py:81
  8.3 20.4 %all-to-all-start = ((bf16[8,2,4,64,128]{4,3,2,1,0:T(8,128)(2,1)}), bf16[8,2,4,64,128]{4,3,2,1,0:T(8,128)(2,1)}, u32[]{:S(2)}, u32[]{:S(2)}) async-start(bf16[8,2,4,64,128]{4,3,2,1,0:T(8,128)(2,1)} %bitcast.1), calls=%async_computation | async-start | bytes 2097152 | tf_op jit(solution)/shard_map/all_to_all | solution.py:67
  12.6 4.8 %copy-start.2 = (bf16[1,128,1024]{2,1,0:T(8,128)(2,1)S(1)}, bf16[1,128,1024]{2,1,0:T(8,128)(2,1)}, u32[]{:S(2)}) copy-start(bf16[1,128,1024]{2,1,0:T(8,128)(2,1)} %param.6) | copy-start | bytes 786436
  17.4 1.6 %copy-start.4 = (s32[4]{0:T(128)S(1)}, s32[4]{0:T(128)}, u32[]{:S(2)}) copy-start(s32[4]{0:T(128)} %param.11) | copy-start | bytes 52
  17.4 1.6 %copy-start.5 = (s32[4]{0:T(128)S(1)}, s32[4]{0:T(128)}, u32[]{:S(2)}) copy-start(s32[4]{0:T(128)} %param.10) | copy-start | bytes 52
  24.9 0.8 %copy-start.1 = (f32[2,128,512]{2,1,0:T(8,128)}, f32[2,128,512]{2,1,0:T(8,128)S(1)}, u32[]{:S(2)}) copy-start(f32[2,128,512]{2,1,0:T(8,128)S(1)} %convolution_bitcast_fusion) | copy-start | bytes 1572868
  26.8 9.6 %collective-permute-start.2 = (bf16[128,512]{1,0:T(8,128)(2,1)S(1)}, bf16[128,512]{1,0:T(8,128)(2,1)S(1)}, u32[]{:S(2)}, u32[]{:S(2)}) collective-permute-start(bf16[128,512]{1,0:T(8,128)(2,1)S(1)} %multiply_convert_fusion.1), channel_id=1, source_target_pairs={{0,4},{4,0},{1,5},{5,1},{2,6},{6,2},{3,7},{7,3},{8,12},{12,8},{9,1... | collective-permute-start | bytes 393224 | tf_op jit(solution)/shard_map/ppermute | solution.py:84
  30.8 5.3 %collective-permute-start.1 = (bf16[128,512]{1,0:T(8,128)(2,1)S(1)}, bf16[128,512]{1,0:T(8,128)(2,1)S(1)}, u32[]{:S(2)}, u32[]{:S(2)}) collective-permute-start(bf16[128,512]{1,0:T(8,128)(2,1)S(1)} %bitcast.68), channel_id=1, source_target_pairs={{0,4},{4,0},{1,5},{5,1},{2,6},{6,2},{3,7},{7,3},{8,12},{12,8},{9,1... | collective-permute-start | bytes 393224 | tf_op jit(solution)/shard_map/ppermute | solution.py:88
  31.0 5.5 %copy-start.3 = (f32[1024]{0:T(1024)S(1)}, f32[1024]{0:T(1024)}, u32[]{:S(2)}) copy-start(f32[1024]{0:T(1024)} %param.9) | copy-start | bytes 12292
where the time goes:
time: 37.8 us; the launch traced here: 37.3 us
  local copies, waits for them, and re-layouts  12.8 us (34%)
  starting transfers between devices  9.38 us (25%)
  other arithmetic  5.31 us (14%)
  matrix products  4.67 us (12%)
  waiting for transfers between devices  4.29 us (11%)
  between operations  0.85 us (2%)
    unnamed x13, local copies, waits for them, and re-layouts  5.58 us
    ppermute x1, waiting for transfers between devices, per_device(): back = lax.ppermute(sent, 'blk', swap)  4.29 us
    all_to_all x1, starting transfers between devices, per_device(): lax.all_to_all(ordered, ('blk', 'store'), split_axis=0, concat_axis=3, ti...  4.24 us
    dot_general x2, matrix products, project(): jnp.einsum('cd,dkh->kch', feats, proj_weight, preferred_element_type=jnp....  3.4 us
    ppermute x1, starting transfers between devices, per_device(): peer = lax.ppermute(mine, 'blk', swap)  2.97 us
    gather x1, local copies, waits for them, and re-layouts, per_device(): ordered = kv_store.at[users].get(mode='promise_in_bounds', unique_indices...  2.66 us
    convert_element_type x2, other arithmetic, project(): gate = jax.nn.silu(proj[1]).astype(jnp.bfloat16)  2.06 us
    reshape x2, local copies, waits for them, and re-layouts, per_device(): ordered = kv_store.at[users].get(mode='promise_in_bounds', unique_indices...  2.02 us
  transfers between devices with their start and end apart: 4, of which 1 were waited for; matrix products, arithmetic and copies ran while one was open for 57% of the time, Pallas kernels for 0%

commit v1 on v0

--- a/solution.py
+++ b/solution.py
@@ -64,7 +64,15 @@
     ordered = jnp.transpose(ordered, (3, 0, 2, 4, 1, 5)).reshape(
         n_blk * n_users, 2, local_heads, n_pos, HEAD_SIZE
     )
-    fetched = lax.all_to_all(ordered, ("blk", "store"), split_axis=0, concat_axis=3, tiled=True)
+    fetched = jnp.concatenate(
+        lax.all_to_all(
+            jnp.stack(jnp.split(ordered, lax.axis_size(("blk", "store")), axis=0)),
+            ("blk", "store"),
+            0,
+            0,
+        ),
+        axis=3,
+    )
     keys = fetched[0, 0]
     values = fetched[0, 1]
     mine = cands[0]

time: 37.8 us -> 42 us (1.11)
  local copies, waits for them, and re-layouts: 12.8 us -> 17.1 us
    unnamed x13 -> x20, local copies, waits for them, and re-layouts: 5.58 us -> 10.2 us
    all_to_all x1 -> x0, local copies, waits for them, and re-layouts: 1.31 us -> none  [per_device(): lax.all_to_all(ordered, ('blk', 'store'), split_axis=0, concat_axis=3, ti...]
    reshape x0 -> x1, local copies, waits for them, and re-layouts: none -> 1.31 us  [per_device(): jnp.concatenate(lax.all_to_all(jnp.stack(jnp.split(ordered, lax.axis_size...]
    reshape x2, local copies, waits for them, and re-layouts: 2.02 us -> 0.98 us  [per_device(): ordered = kv_store.at[users].get(mode='promise_in_bounds', unique_indices...]
    another operation x0 -> x1, local copies, waits for them, and re-layouts: none -> 0.65 us  [per_device(): jnp.stack(jnp.split(ordered, lax.axis_size(('blk', 'store')), axis=0))]
  transfers between devices with their start and end apart: 4 -> 4, of which waited for: 1 -> 1; matrix products, arithmetic and copies ran while one was open for 57% -> 61% of each run, Pallas kernels for 0% -> 0%
where the time goes in v1:
time: 42 us; the launch traced here: 41.6 us
  local copies, waits for them, and re-layouts  17.1 us (41%)
  starting transfers between devices  9.38 us (22%)
  other arithmetic  5.31 us (13%)
  matrix products  4.67 us (11%)
  waiting for transfers between devices  4.29 us (10%)
  between operations  0.87 us (2%)
    unnamed x20, local copies, waits for them, and re-layouts  10.2 us
    ppermute x1, waiting for transfers between devices, per_device(): back = lax.ppermute(sent, 'blk', swap)  4.29 us
    all_to_all x1, starting transfers between devices, per_device(): lax.all_to_all(jnp.stack(jnp.split(ordered, lax.axis_size(('blk', 'store'...  4.24 us
    dot_general x2, matrix products, project(): jnp.einsum('cd,dkh->kch', feats, proj_weight, preferred_element_type=jnp....  3.39 us
    ppermute x1, starting transfers between devices, per_device(): peer = lax.ppermute(mine, 'blk', swap)  2.97 us
    gather x1, local copies, waits for them, and re-layouts, per_device(): ordered = kv_store.at[users].get(mode='promise_in_bounds', unique_indices...  2.66 us
    convert_element_type x2, other arithmetic, project(): gate = jax.nn.silu(proj[1]).astype(jnp.bfloat16)  2.06 us
    ppermute x1, starting transfers between devices, per_device(): gate_back = lax.ppermute(gate_peer, 'blk', swap)  1.96 us
  transfers between devices with their start and end apart: 4, of which 1 were waited for; matrix products, arithmetic and copies ran while one was open for 61% of the time, Pallas kernels for 0%

profile of v1, /device:TPU:0, one launch (start us, length us, event | category | flops | bytes accessed | tf_op | source)
XLA Modules:
  0.0 41.6 jit_solution(1324373473761873469)
XLA Ops:
  0.0 3.0 %collective-permute-start = (bf16[128,1024]{1,0:T(8,128)(2,1)}, bf16[128,1024]{1,0:T(8,128)(2,1)}, u32[]{:S(2)}, u32[]{:S(2)}) collective-permute-start(bf16[128,1024]{1,0:T(8,128)(2,1)} %bitcast.104), channel_id=1, source_target_pairs={{0,4},{4,0},{1,5},{5,1},{2,6},{6,2},{3,7},{7,3},{8,12},{12,8},{9,1... | collective-permute-start | bytes 786440 | tf_op jit(solution)/shard_map/ppermute | solution.py:89
  3.0 0.7 %compare_select_fusion = s32[4]{0:T(128)S(1)} fusion(s32[4]{0:T(128)} %param.10), kind=kLoop, calls=%fused_computation.58 | loop fusion | flops 12 | bytes 32 | tf_op jit(solution)/shard_map/select_n | solution.py:61
  3.6 2.7 %gather_fusion = bf16[4,64,2,1024]{3,2,1,0:T(2,128)(2,1)S(1)} fusion(bf16[4,64,2,1024]{3,2,1,0:T(2,128)(2,1)S(1)} %copy-done, s32[1024]{0:T(1024)S(1)} %pad_clamp_fusion), kind=kCustom, calls=%fused_computation | custom fusion | bytes 2097168 | tf_op jit(solution)/shard_map/gather | solution.py:61
  6.3 0.7 %reshape.237 = bf16[4,64,2,2,4,128]{5,4,3,2,1,0:T(4,128)(2,1)S(1)} reshape(bf16[4,64,2,1024]{3,2,1,0:T(2,128)(2,1)S(1)} %gather_fusion) | data formatting | bytes 2097152 | tf_op jit(solution)/shard_map/reshape | solution.py:62
  7.3 0.7 %fusion.20 = bf16[8,1,2,4,64,128]{5,4,3,2,1,0:T(8,128)(2,1)} fusion(bf16[8,2,4,64,128]{4,3,2,1,0:T(8,128)(2,1)S(1)} %bitcast.91), kind=kLoop, calls=%fused_computation.53 | loop fusion | bytes 262144
  8.0 0.7 %fusion.19 = bf16[8,1,2,4,64,128]{5,4,3,2,1,0:T(8,128)(2,1)} fusion(bf16[8,1,2,4,64,128]{5,4,3,2,1,0:T(8,128)(2,1)} %fusion.20, bf16[8,2,4,64,128]{4,3,2,1,0:T(8,128)(2,1)S(1)} %bitcast.92), kind=kLoop, calls=%fused_computation.51 | loop fusion | bytes 262144
  8.6 0.7 %fusion.18 = bf16[8,1,2,4,64,128]{5,4,3,2,1,0:T(8,128)(2,1)} fusion(bf16[8,1,2,4,64,128]{5,4,3,2,1,0:T(8,128)(2,1)} %fusion.19, bf16[8,2,4,64,128]{4,3,2,1,0:T(8,128)(2,1)S(1)} %bitcast.93), kind=kLoop, calls=%fused_computation.49 | loop fusion | bytes 262144
  9.9 0.7 %fusion.16 = bf16[8,1,2,4,64,128]{5,4,3,2,1,0:T(8,128)(2,1)} fusion(bf16[8,1,2,4,64,128]{5,4,3,2,1,0:T(8,128)(2,1)} %fusion.17, bf16[8,2,4,64,128]{4,3,2,1,0:T(8,128)(2,1)S(1)} %bitcast.95), kind=kLoop, calls=%fused_computation.45 | loop fusion | bytes 262144
  10.6 0.7 %fusion.15 = bf16[8,1,2,4,64,128]{5,4,3,2,1,0:T(8,128)(2,1)} fusion(bf16[8,1,2,4,64,128]{5,4,3,2,1,0:T(8,128)(2,1)} %fusion.16, bf16[8,2,4,64,128]{4,3,2,1,0:T(8,128)(2,1)S(1)} %bitcast.96), kind=kLoop, calls=%fused_computation.43 | loop fusion | bytes 262144
  11.3 0.7 %fusion.14 = bf16[8,1,2,4,64,128]{5,4,3,2,1,0:T(8,128)(2,1)} fusion(bf16[8,1,2,4,64,128]{5,4,3,2,1,0:T(8,128)(2,1)} %fusion.15, bf16[8,2,4,64,128]{4,3,2,1,0:T(8,128)(2,1)S(1)} %bitcast.97), kind=kLoop, calls=%fused_computation.41 | loop fusion | bytes 262144
  11.9 0.7 %fusion.13 = bf16[8,1,2,4,64,128]{5,4,3,2,1,0:T(8,128)(2,1)} fusion(bf16[8,1,2,4,64,128]{5,4,3,2,1,0:T(8,128)(2,1)} %fusion.14, bf16[8,2,4,64,128]{4,3,2,1,0:T(8,128)(2,1)S(1)} %bitcast.98), kind=kLoop, calls=%fused_computation.39 | loop fusion | bytes 262144 | tf_op jit(solution)/shard_map/stack | solution.py:69
  12.6 4.2 %all-to-all-start = ((bf16[8,1,2,4,64,128]{5,4,3,2,1,0:T(8,128)(2,1)}), bf16[8,1,2,4,64,128]{5,4,3,2,1,0:T(8,128)(2,1)}, u32[]{:S(2)}, u32[]{:S(2)}) async-start(bf16[8,1,2,4,64,128]{5,4,3,2,1,0:T(8,128)(2,1)} %fusion.13), calls=%async_computation | async-start | bytes 2097152 | tf_op jit(solution)/shard_map/all_to_all | solution.py:68
  16.9 4.8 %copy.35 = bf16[1024,2,512]{0,2,1:T(8,128)(2,1)S(1)} copy(bf16[1024,2,512]{2,1,0:T(2,128)(2,1)} %param.8) | data formatting | bytes 4194304 | tf_op args[2]
  21.7 1.6 %convolution_bitcast_fusion.1 = f32[2,128,512]{2,1,0:T(8,128)} fusion(bf16[1024,2,512]{0,2,1:T(8,128)(2,1)S(1)} %copy.35, bf16[1,128,1024]{2,1,0:T(8,128)(2,1)S(1)} %copy-done.2), kind=kOutput, calls=%fused_computation.4 | convolution fusion | flops 268435456 | bytes 2883584 | tf_op jit(solution)/shard_map/cd,dkh->kch/dot_general | solution.py:82
  23.3 0.7 %select_reduce_fusion = s32[]{:T(128)} fusion(s32[4]{0:T(128)S(1)} %copy-done.4, s32[4]{0:T(128)S(1)} %copy-done.5, pred[4]{0:T(512)(128)(4,1)S(1)} %iota_compare_fusion.2), kind=kLoop, calls=%fused_computation.59 | loop fusion | flops 63 | bytes 40 | tf_op jit(solution)/shard_map/reduce_sum | solution.py:55
  25.3 1.0 %slice.51 = bf16[1,128,512]{2,1,0:T(8,128)(2,1)S(1)} slice(f32[2,128,512]{2,1,0:T(8,128)} %convolution_bitcast_fusion.1), slice={[0:1], [0:128], [0:512]} | slice | bytes 262144 | tf_op jit(solution)/shard_map/slice | solution.py:83
  26.4 1.0 %multiply_convert_fusion.2 = bf16[128,512]{1,0:T(8,128)(2,1)S(1)} fusion(f32[2,128,512]{2,1,0:T(8,128)} %convolution_bitcast_fusion.1), kind=kLoop, calls=%fused_computation.35 | loop fusion | flops 327680 | bytes 393216 | tf_op jit(solution)/shard_map/convert_element_type | solution.py:84
  27.4 1.8 %convolution_bitcast_fusion = f32[2,128,512]{2,1,0:T(8,128)S(1)} fusion(bf16[1024,2,512]{0,2,1:T(8,128)(2,1)S(1)} %copy.35, bf16[128,1024]{1,0:T(8,128)(2,1)} %collective-permute-done), kind=kOutput, calls=%fused_computation.3 | convolution fusion | flops 268435456 | bytes 2883584 | tf_op jit(solution)/shard_map/cd,dkh->kch/dot_general | solution.py:82
  29.2 0.8 %copy-done.1 = f32[2,128,512]{2,1,0:T(8,128)} copy-done((f32[2,128,512]{2,1,0:T(8,128)}, f32[2,128,512]{2,1,0:T(8,128)S(1)}, u32[]{:S(2)}) %copy-start.1) | copy-done | bytes 524312
  30.0 1.0 %multiply_convert_fusion.1 = bf16[128,512]{1,0:T(8,128)(2,1)S(1)} fusion(f32[2,128,512]{2,1,0:T(8,128)} %copy-done.1), kind=kLoop, calls=%fused_computation.34 | loop fusion | flops 327680 | bytes 393216 | tf_op jit(solution)/shard_map/convert_element_type | solution.py:84
  31.1 2.0 %collective-permute-start.2 = (bf16[128,512]{1,0:T(8,128)(2,1)S(1)}, bf16[128,512]{1,0:T(8,128)(2,1)S(1)}, u32[]{:S(2)}, u32[]{:S(2)}) collective-permute-start(bf16[128,512]{1,0:T(8,128)(2,1)S(1)} %multiply_convert_fusion.1), channel_id=1, source_target_pairs={{0,4},{4,0},{1,5},{5,1},{2,6},{6,2},{3,7},{7,3},{8,12},{12,8},{9,1... | collective-permute-start | bytes 393224 | tf_op jit(solution)/shard_map/ppermute | solution.py:92
  33.0 1.3 %copy.34 = bf16[1,2,4,8,64,128]{5,4,3,2,1,0:T(8,128)(2,1)S(1)} copy(bf16[1,2,4,8,64,128]{5,4,2,1,0,3:T(8,128)(2,1)} %bitcast.11) | data formatting | bytes 2097152 | tf_op jit(solution)/shard_map/reshape | solution.py:67
  36.1 4.3 %collective-permute-done.1 = bf16[128,512]{1,0:T(8,128)(2,1)S(1)} collective-permute-done((bf16[128,512]{1,0:T(8,128)(2,1)S(1)}, bf16[128,512]{1,0:T(8,128)(2,1)S(1)}, u32[]{:S(2)}, u32[]{:S(2)}) %collective-permute-start.1) | collective-permute-done | bytes 131104 | tf_op jit(solution)/shard_map/ppermute | solution.py:96
  40.7 0.9 %multiply_convert_fusion = bf16[1,128,1024]{2,1,0:T(8,128)(2,1)} fusion(bf16[1,128,512]{2,1,0:T(8,128)(2,1)S(1)} %bitcast.99, bf16[1,128,512]{2,1,0:T(8,128)(2,1)S(1)} %concatenate.52, bf16[1,128,512]{2,1,0:T(8,128)(2,1)S(1)} %bitcast.107, bf16[1,128,512]{2,1,0:T(8,128)(2,1)S(1)} %bitcast.102, f32[1024]{0:T(1024)S(1)} %copy-done.3, ...), kind=kLoop, calls=%fused_computation.16 | loop fusion | flops 3276800 | bytes 791553 | tf_op jit(solution)/shard_map/convert_element_type | solution.py:46
  (34 shorter events, 3.8 us)
Async XLA Ops:
  0.0 3.6 %copy-start = (bf16[4,64,2,1024]{3,2,1,0:T(2,128)(2,1)S(1)}, bf16[4,64,2,1024]{3,2,1,0:T(2,128)(2,1)}, u32[]{:S(2)}) copy-start(bf16[4,64,2,1024]{3,2,1,0:T(2,128)(2,1)} %param.7) | copy-start | bytes 3145732
  0.0 27.4 %collective-permute-start = (bf16[128,1024]{1,0:T(8,128)(2,1)}, bf16[128,1024]{1,0:T(8,128)(2,1)}, u32[]{:S(2)}, u32[]{:S(2)}) collective-permute-start(bf16[128,1024]{1,0:T(8,128)(2,1)} %bitcast.104), channel_id=1, source_target_pairs={{0,4},{4,0},{1,5},{5,1},{2,6},{6,2},{3,7},{7,3},{8,12},{12,8},{9,1... | collective-permute-start | bytes 786440 | tf_op jit(solution)/shard_map/ppermute | solution.py:89
  12.6 20.4 %all-to-all-start = ((bf16[8,1,2,4,64,128]{5,4,3,2,1,0:T(8,128)(2,1)}), bf16[8,1,2,4,64,128]{5,4,3,2,1,0:T(8,128)(2,1)}, u32[]{:S(2)}, u32[]{:S(2)}) async-start(bf16[8,1,2,4,64,128]{5,4,3,2,1,0:T(8,128)(2,1)} %fusion.13), calls=%async_computation | async-start | bytes 2097152 | tf_op jit(solution)/shard_map/all_to_all | solution.py:68
  16.8 4.8 %copy-start.2 = (bf16[1,128,1024]{2,1,0:T(8,128)(2,1)S(1)}, bf16[1,128,1024]{2,1,0:T(8,128)(2,1)}, u32[]{:S(2)}) copy-start(bf16[1,128,1024]{2,1,0:T(8,128)(2,1)} %param.6) | copy-start | bytes 786436
  21.7 1.6 %copy-start.4 = (s32[4]{0:T(128)S(1)}, s32[4]{0:T(128)}, u32[]{:S(2)}) copy-start(s32[4]{0:T(128)} %param.11) | copy-start | bytes 52
  21.7 1.6 %copy-start.5 = (s32[4]{0:T(128)S(1)}, s32[4]{0:T(128)}, u32[]{:S(2)}) copy-start(s32[4]{0:T(128)} %param.10) | copy-start | bytes 52
  29.2 0.8 %copy-start.1 = (f32[2,128,512]{2,1,0:T(8,128)}, f32[2,128,512]{2,1,0:T(8,128)S(1)}, u32[]{:S(2)}) copy-start(f32[2,128,512]{2,1,0:T(8,128)S(1)} %convolution_bitcast_fusion) | copy-start | bytes 1572868
  31.1 9.7 %collective-permute-start.2 = (bf16[128,512]{1,0:T(8,128)(2,1)S(1)}, bf16[128,512]{1,0:T(8,128)(2,1)S(1)}, u32[]{:S(2)}, u32[]{:S(2)}) collective-permute-start(bf16[128,512]{1,0:T(8,128)(2,1)S(1)} %multiply_convert_fusion.1), channel_id=1, source_target_pairs={{0,4},{4,0},{1,5},{5,1},{2,6},{6,2},{3,7},{7,3},{8,12},{12,8},{9,1... | collective-permute-start | bytes 393224 | tf_op jit(solution)/shard_map/ppermute | solution.py:92
  35.0 5.3 %collective-permute-start.1 = (bf16[128,512]{1,0:T(8,128)(2,1)S(1)}, bf16[128,512]{1,0:T(8,128)(2,1)S(1)}, u32[]{:S(2)}, u32[]{:S(2)}) collective-permute-start(bf16[128,512]{1,0:T(8,128)(2,1)S(1)} %bitcast.106), channel_id=1, source_target_pairs={{0,4},{4,0},{1,5},{5,1},{2,6},{6,2},{3,7},{7,3},{8,12},{12,8},{9,1... | collective-permute-start | bytes 393224 | tf_op jit(solution)/shard_map/ppermute | solution.py:96
  35.2 5.5 %copy-start.3 = (f32[1024]{0:T(1024)S(1)}, f32[1024]{0:T(1024)}, u32[]{:S(2)}) copy-start(f32[1024]{0:T(1024)} %param.9) | copy-start | bytes 12292
